TPU v7x, 128 devices: a whole 4x4x4 slice. The times are simulated.
128 devices in a mesh: blk: 2 (over x_lo), tile: 64 (over z, y, x_hi, core).
Axes of the slice: x: 4 (x_hi: 2, x_lo: 2; x = x_hi * 2 + x_lo), y: 4, z: 4, core: 2. Of those that a mesh axis runs over, the one named last changes fastest.
Arguments:
- forward: float32 [2, 1024, 65536], P(None, 'blk', 'tile'), may hold values from -6 to 6
- backward: float32 [2, 1024, 65536], P(None, 'blk', 'tile'), may hold values from -6 to 6
- phase: float32 [64, 1024], P('tile'), may hold values from -3.140625 to 3.140625
- footprint: int32 [16, 64], P('blk', 'tile'), may hold values 0 or 1
- groups: int32 [1024], replicated, may hold values from 0 to 44
Outputs:
- margin: float32 [2, 1024, 1024], P(None, 'blk', 'tile')
- gradient: float32 [64, 1024], P('tile', 'blk')
All inputs are finite; a program needn't handle non-finite values. No bound on the sum of `footprint` on one device may be relied on, other than what follows from the above.
Results may differ from a plain program's by a relative error of at most 0.00016.
Values sent between devices are 32-bit elements; how exact they have to be, the bound alone decides.
No kernel may reach another device: no remote copies, remote signals or barrier semaphores. Data moves between devices by JAX's collectives and lax.ppermute only.
A program may use at most 320 MiB of HBM per device.

v0:
```python
import math

import jax
import jax.numpy as jnp
from jax import lax
from jax.sharding import PartitionSpec as P

MODES = 1024
BLOCK = 64


highest = lax.Precision.HIGHEST
cross_weight = 0.05


def pair_margin(left_fields, right_fields):
    left_count = left_fields.shape[1]
    right_count = right_fields.shape[1]
    stacked = lax.dot_general(
        left_fields.reshape(2 * left_count, -1),
        right_fields.reshape(2 * right_count, -1),
        (((1,), (1,)), ((), ())),
        precision=highest,
        preferred_element_type=jnp.float32,
    )
    real_part = stacked[:left_count, :right_count] + stacked[left_count:, right_count:]
    imag_part = stacked[:left_count, right_count:] - stacked[left_count:, :right_count]
    return jnp.stack([real_part, imag_part])


def response(coupled, fields):
    source_count = coupled.shape[1]
    target_count = coupled.shape[2]
    mixing = jnp.stack(
        [
            jnp.concatenate([coupled[0], -coupled[1]], 0),
            jnp.concatenate([coupled[1], coupled[0]], 0),
        ],
        axis=2,
    ).reshape(2 * source_count, 2 * target_count)
    product = lax.dot_general(
        mixing,
        fields.reshape(2 * source_count, -1),
        (((0,), (0,)), ((), ())),
        precision=highest,
        preferred_element_type=jnp.float32,
    )
    return product.reshape(target_count, 2, -1)


def margin_rows(masked, portion):
    return pair_margin(masked, portion)


def response_rows(coupled_rows, masked):
    return response(coupled_rows, masked)


def body(forward, backward, phase, footprint, groups):
    local_modes = backward.shape[1]
    pixel_count = backward.shape[2]
    rows_here, width_here = phase.shape
    phase_cos = jnp.cos(phase).reshape(pixel_count)
    phase_sin = jnp.sin(phase).reshape(pixel_count)
    shifted = jnp.stack(
        [
            forward[0] * phase_cos - forward[1] * phase_sin,
            forward[0] * phase_sin + forward[1] * phase_cos,
        ]
    )
    tile_count = lax.axis_size("tile")
    inverse_root = 1.0 / math.sqrt(pixel_count * tile_count)
    grad_scale = 0.25 / math.sqrt(MODES)
    column_share = MODES // tile_count
    tile_offset = lax.axis_index("tile") * column_share
    mode_offset = lax.axis_index("blk") * local_modes
    row_gate = jnp.repeat(footprint[:, 0].astype(jnp.float32), BLOCK)
    masked = backward * row_gate[None, :, None]
    block_values = margin_rows(masked, lax.all_gather(shifted, "blk", axis=1, tiled=True))
    margin_full = lax.psum(block_values, "tile") * inverse_root
    margin_out = lax.dynamic_slice_in_dim(margin_full, tile_offset, column_share, 2)
    own_groups = lax.dynamic_slice_in_dim(groups, mode_offset, local_modes)
    weights = jnp.where(own_groups[:, None] == groups[None, :], 1.0, -cross_weight).astype(
        jnp.float32
    )
    coupled = margin_full * weights[None]
    portion = lax.all_gather(shifted, "blk", axis=1, tiled=True)
    reply = response_rows(coupled, masked)
    local_sum = jnp.sum(portion[1] * reply[:, 0] - portion[0] * reply[:, 1], axis=0)
    gradient = (
        lax.psum_scatter(
            local_sum.reshape(rows_here, width_here), "blk", scatter_dimension=1, tiled=True
        )
        * grad_scale
    )
    return (margin_out, gradient)


def solution(mesh):
    placed = (
        P(None, "blk", "tile"),
        P(None, "blk", "tile"),
        P("tile", None),
        P("blk", "tile"),
        P(),
    )
    return jax.shard_map(
        body,
        mesh=mesh,
        in_specs=placed,
        out_specs=(P(None, "blk", "tile"), P("tile", "blk")),
        check_vma=False,
    )
```

profile of v0, /device:TPU:1, one launch (start us, length us, event | category | flops | bytes accessed | tf_op | source)
XLA Modules:
  0.0 919.9 jit_solution(1338231969495644198)
XLA Ops:
  7.2 0.0 all-gather.2.cloned.1.call-start
  7.2 0.8 fusion.9
  8.0 2.8 multiply_subtract_fusion
  10.8 2.3 pad_maximum_fusion.1
  13.1 0.0 copy-start.1
  13.1 0.0 all-gather.2.cloned.1.call-update
  13.1 0.0 all-reduce.2.cloned.1.call-start
  13.2 0.6 copy-done.1
  13.8 0.1 broadcast_in_dim.14
  13.9 0.1 mul.82
  13.9 4.4 broadcast_multiply_fusion.1
  18.4 104.4 %all-gather.2.cloned.1.call-done = f32[2,1024,1024]{2,1,0:T(8,128)} async-done(((f32[2,512,1024]{2,1,0:T(8,128)}), f32[2,1024,1024]{2,1,0:T(8,128)}) %all-gather.2.cloned.1.call-update) | async-done | bytes 8388624 | tf_op jit(solution)/shard_map/all_gather | solution.py:79
  122.8 29.7 %fusion.10 = f32[1024,2048]{1,0:T(8,128)S(1)} fusion(f32[1024,1024]{1,0:T(8,128)} %bitcast.55, f32[2048,1024]{1,0:T(8,128)} %bitcast.54), kind=kOutput, calls=%fused_computation.31 | convolution fusion | flops 25769803776 | bytes 20971520 | tf_op jit(solution)/shard_map/dot_general | solution.py:19
  152.6 1.4 fusion.7
  153.9 2.3 pad_maximum_fusion.2
  156.2 0.0 copy-start
  156.2 0.0 all-reduce.2.cloned.1.call-update
  156.2 0.2 reduce-scatter.4.cloned.1.call-start
  156.5 0.4 copy-done
  156.9 0.1 dynamic_slice.7
  157.0 0.3 select_multiply_fusion
  157.3 650.5 %all-reduce.2.cloned.1.call-done = f32[2,512,1024]{2,1,0:T(8,128)} async-done(((f32[2,512,1024]{2,1,0:T(8,128)}), f32[2,512,1024]{2,1,0:T(8,128)}) %all-reduce.2.cloned.1.call-update) | async-done | bytes 4194320 | tf_op jit(solution)/shard_map/psum | solution.py:80
  807.8 2.9 broadcast_multiply_fusion
  810.6 0.2 fusion.8
  810.8 1.7 slice_bitcast_fusion.4
  812.5 3.5 maximum_bitcast_fusion
  816.0 4.1 pad_maximum_fusion
  820.0 13.4 %copy.11 = f32[1024,1024,2]{0,2,1:T(2,128)} copy(f32[1024,1024,2]{1,0,2:T(8,128)} %pad_maximum_fusion) | data formatting | bytes 16777216 | tf_op jit(solution)/shard_map/stack | solution.py:34
  833.4 10.9 %reshape.75 = f32[1024,2048]{0,1:T(8,128)} reshape(f32[1024,1024,2]{0,2,1:T(2,128)} %copy.11) | data formatting | bytes 16777216 | tf_op jit(solution)/shard_map/reshape | solution.py:40
  844.3 10.6 %dot_general.12 = f32[1024,2,1024]{2,1,0:T(2,128)} reshape(f32[2048,1024]{1,0:T(8,128)} %bitcast.53) | data formatting | bytes 16777216 | tf_op jit(solution)/shard_map/dot_general | solution.py:41
  854.9 33.2 %fusion = f32[1024,2,1024]{2,0,1:T(8,128)S(1)} fusion(f32[1024,1024,1]{1,0,2:T(8,128)} %bitcast.56, f32[1024,2,1024]{2,1,0:T(2,128)} %dot_general.12), kind=kOutput, calls=%fused_computation.1 | convolution fusion | flops 25769803776 | bytes 20971520 | tf_op jit(solution)/shard_map/dot_general | solution.py:41
  888.1 4.7 fusion.4
  892.8 1.0 copy.14
  893.8 0.0 reduce-scatter.4.cloned.1.call-update
  893.8 1.3 dynamic-slice_multiply_fusion
  895.1 0.8 copy.13
  895.9 15.8 %reduce-scatter.4.cloned.1.call-done = f32[512,1]{1,0:T(8,128)} async-done(((f32[1024,1]{1,0:T(8,128)}), f32[512,1]{1,0:T(8,128)}) %reduce-scatter.4.cloned.1.call-update) | async-done | bytes 2064
  911.7 1.1 copy.15
  912.8 0.6 broadcast_multiply_fusion.2
  (1 shorter events, 0.0 us)
Async XLA Ops:
  7.2 115.7 %all-gather.2.cloned.1.call-start = ((), (), s32[]{:S(2)}) async-start(), calls=%async_computation.1 | async-start | bytes 12582912 | tf_op jit(solution)/shard_map/all_gather | solution.py:79
  13.1 0.7 copy-start.1
  13.1 794.6 %all-reduce.2.cloned.1.call-start = ((), (), s32[]{:S(2)}) async-start(), calls=%async_computation.2 | async-start | bytes 8388608 | tf_op jit(solution)/shard_map/psum | solution.py:80
  156.2 0.7 copy-start
  156.2 755.5 %reduce-scatter.4.cloned.1.call-start = ((), (), s32[]{:S(2)}) async-start(), calls=%async_computation.3 | async-start | bytes 786432
Sparse Core Ops, SparseCore 0:
  13.3 109.5 all-gather.1
  156.4 651.3 all-reduce.1
  894.0 17.7 reduce-scatter.3
where the time goes:
time: 921 us; the launch traced here: 920 us
  waiting for transfers between devices  771 us (84%)
  matrix products  63 us (7%)
  local copies, waits for them, and re-layouts  41.4 us (4%)
  other arithmetic  30.6 us (3%)
  between operations  13.8 us (1%)
    psum x1, waiting for transfers between devices, body(): margin_full = lax.psum(block_values, 'tile') * inverse_root  651 us
    all_gather x1, waiting for transfers between devices, body(): lax.all_gather(shifted, 'blk', axis=1, tiled=True)  104 us
    dot_general x1, matrix products, response(): lax.dot_general(mixing, fields.reshape(2 * source_count, -1), (((0,), (0,...  33.2 us
    dot_general x1, matrix products, pair_margin(): lax.dot_general(left_fields.reshape(2 * left_count, -1), right_fields.res...  29.7 us
  transfers between devices with their start and end apart: 3, of which 3 were waited for; matrix products, arithmetic and copies ran while one was open for 1% of the time, Pallas kernels for 0%

commit v1 on v0

--- a/solution.py
+++ b/solution.py
@@ -1,6 +1,7 @@
 import math
 
 import jax
+import numpy as np
 import jax.numpy as jnp
 from jax import lax
 from jax.sharding import PartitionSpec as P
@@ -9,6 +10,7 @@
 BLOCK = 64
 
 
+TILE = ("z", "y", "xh", "core")
 highest = lax.Precision.HIGHEST
 cross_weight = 0.05
 
@@ -56,6 +58,15 @@
     return response(coupled_rows, masked)
 
 
+def tile_sum(values):
+    rows = values.reshape(-1, values.shape[-1])
+    for axes in ("core", ("z", "y"), "xh"):
+        rows = lax.psum_scatter(rows, axes, scatter_dimension=0, tiled=True)
+    for axes in ("xh", ("z", "y"), "core"):
+        rows = lax.all_gather(rows, axes, axis=0, tiled=True)
+    return rows.reshape(values.shape)
+
+
 def body(forward, backward, phase, footprint, groups):
     local_modes = backward.shape[1]
     pixel_count = backward.shape[2]
@@ -68,16 +79,16 @@
             forward[0] * phase_sin + forward[1] * phase_cos,
         ]
     )
-    tile_count = lax.axis_size("tile")
+    tile_count = lax.axis_size(TILE)
     inverse_root = 1.0 / math.sqrt(pixel_count * tile_count)
     grad_scale = 0.25 / math.sqrt(MODES)
     column_share = MODES // tile_count
-    tile_offset = lax.axis_index("tile") * column_share
+    tile_offset = lax.axis_index(TILE) * column_share
     mode_offset = lax.axis_index("blk") * local_modes
     row_gate = jnp.repeat(footprint[:, 0].astype(jnp.float32), BLOCK)
     masked = backward * row_gate[None, :, None]
     block_values = margin_rows(masked, lax.all_gather(shifted, "blk", axis=1, tiled=True))
-    margin_full = lax.psum(block_values, "tile") * inverse_root
+    margin_full = tile_sum(block_values) * inverse_root
     margin_out = lax.dynamic_slice_in_dim(margin_full, tile_offset, column_share, 2)
     own_groups = lax.dynamic_slice_in_dim(groups, mode_offset, local_modes)
     weights = jnp.where(own_groups[:, None] == groups[None, :], 1.0, -cross_weight).astype(
@@ -96,18 +107,25 @@
     return (margin_out, gradient)
 
 
+def fine_mesh(mesh):
+    devices = np.asarray(mesh.devices)
+    blk, tile = devices.shape
+    return jax.sharding.Mesh(devices.reshape(blk, 4, tile // 16, 2, 2), ("blk",) + TILE)
+
+
 def solution(mesh):
+    mesh = fine_mesh(mesh)
     placed = (
-        P(None, "blk", "tile"),
-        P(None, "blk", "tile"),
-        P("tile", None),
-        P("blk", "tile"),
+        P(None, "blk", TILE),
+        P(None, "blk", TILE),
+        P(TILE, None),
+        P("blk", TILE),
         P(),
     )
     return jax.shard_map(
         body,
         mesh=mesh,
         in_specs=placed,
-        out_specs=(P(None, "blk", "tile"), P("tile", "blk")),
+        out_specs=(P(None, "blk", TILE), P(TILE, "blk")),
         check_vma=False,
     )

time: 921 us -> 451 us (0.49)
  waiting for transfers between devices: 771 us -> 295 us
    psum x1 -> x0, waiting for transfers between devices: 651 us -> none  [body(): margin_full = lax.psum(block_values, 'tile') * inverse_root]
    reduce_scatter x0 -> x3, waiting for transfers between devices: none -> 112 us  [tile_sum(): rows = lax.psum_scatter(rows, axes, scatter_dimension=0, tiled=True)]
    all_gather x0 -> x2, waiting for transfers between devices: none -> 63.2 us  [tile_sum(): rows = lax.all_gather(rows, axes, axis=0, tiled=True)]
  transfers between devices with their start and end apart: 3 -> 7, of which waited for: 3 -> 7; matrix products, arithmetic and copies ran while one was open for 1% -> 2% of each run, Pallas kernels for 0% -> 0%
where the time goes in v1:
time: 451 us; the launch traced here: 450 us
  waiting for transfers between devices  295 us (65%)
  matrix products  63 us (14%)
  local copies, waits for them, and re-layouts  41 us (9%)
  other arithmetic  30.6 us (7%)
  between operations  14.2 us (3%)
  blocking collectives  5.59 us (1%)
    reduce_scatter x3, waiting for transfers between devices, tile_sum(): rows = lax.psum_scatter(rows, axes, scatter_dimension=0, tiled=True)  112 us
    all_gather x1, waiting for transfers between devices, body(): lax.all_gather(shifted, 'blk', axis=1, tiled=True)  104 us
    all_gather x2, waiting for transfers between devices, tile_sum(): rows = lax.all_gather(rows, axes, axis=0, tiled=True)  63.2 us
    dot_general x1, matrix products, response(): lax.dot_general(mixing, fields.reshape(2 * source_count, -1), (((0,), (0,...  33.2 us
    dot_general x1, matrix products, pair_margin(): lax.dot_general(left_fields.reshape(2 * left_count, -1), right_fields.res...  29.7 us
    unnamed x8, waiting for transfers between devices  16.1 us
    another operation x1, local copies, waits for them, and re-layouts, response(): jnp.stack([jnp.concatenate([coupled[0], -coupled[1]], 0), jnp.concatenate...  13.3 us
    reshape x1, local copies, waits for them, and re-layouts, response(): mixing = jnp.stack([jnp.concatenate([coupled[0], -coupled[1]], 0), jnp.co...  10.9 us
  transfers between devices with their start and end apart: 7, of which 7 were waited for; matrix products, arithmetic and copies ran while one was open for 2% of the time, Pallas kernels for 0%

profile of v1, /device:TPU:1, one launch (start us, length us, event | category | flops | bytes accessed | tf_op | source)
XLA Modules:
  0.0 450.1 jit_solution(3743706317775255586)
XLA Ops:
  7.2 0.0 all-gather.4.cloned.1.call-start
  7.2 0.8 fusion.9
  8.0 2.8 multiply_subtract_fusion
  10.8 2.3 pad_maximum_fusion.1
  13.1 0.0 copy-start.1
  13.1 0.0 all-gather.4.cloned.1.call-update
  13.2 0.0 reduce-scatter.7.cloned.1.call-start
  13.2 0.6 copy-done.1
  13.8 0.1 broadcast_in_dim.14
  13.9 0.1 mul.91
  13.9 4.5 broadcast_multiply_fusion.1
  18.4 104.4 %all-gather.4.cloned.1.call-done = f32[2,1024,1024]{2,1,0:T(8,128)} async-done(((f32[2,512,1024]{2,1,0:T(8,128)}), f32[2,1024,1024]{2,1,0:T(8,128)}) %all-gather.4.cloned.1.call-update) | async-done | bytes 8388624 | tf_op jit(solution)/shard_map/all_gather | solution.py:90
  122.8 29.7 %fusion.10 = f32[1024,2048]{1,0:T(8,128)S(1)} fusion(f32[1024,1024]{1,0:T(8,128)} %bitcast.60, f32[2048,1024]{1,0:T(8,128)} %bitcast.57), kind=kOutput, calls=%fused_computation.31 | convolution fusion | flops 25769803776 | bytes 20971520 | tf_op jit(solution)/shard_map/dot_general | solution.py:21
  152.6 1.4 fusion.7
  154.0 2.3 pad_maximum_fusion.2
  156.2 0.0 copy-start
  156.2 0.0 reduce-scatter.7.cloned.1.call-update
  156.3 0.0 reduce-scatter.9.cloned.1.call-start
  156.3 16.4 %reduce-scatter.7.cloned.1.call-done = f32[512,1024]{1,0:T(8,128)} async-done(((f32[1024,1024]{1,0:T(8,128)}), f32[512,1024]{1,0:T(8,128)}) %reduce-scatter.7.cloned.1.call-update) | async-done | bytes 2097168 | tf_op jit(solution)/shard_map/reduce_scatter | solution.py:64
  172.7 0.0 reduce-scatter.9.cloned.1.call-update
  172.7 0.0 reduce-scatter.11.cloned.1.call-start
  172.8 78.1 %reduce-scatter.9.cloned.1.call-done = f32[32,1024]{1,0:T(8,128)} async-done(((f32[512,1024]{1,0:T(8,128)}), f32[32,1024]{1,0:T(8,128)}) %reduce-scatter.9.cloned.1.call-update) | async-done | bytes 131088 | tf_op jit(solution)/shard_map/reduce_scatter | solution.py:64
  250.9 0.0 reduce-scatter.11.cloned.1.call-update
  250.9 0.0 all-gather.6.cloned.1.call-start
  250.9 17.1 %reduce-scatter.11.cloned.1.call-done = f32[16,1024]{1,0:T(8,128)} async-done(((f32[32,1024]{1,0:T(8,128)}), f32[16,1024]{1,0:T(8,128)}) %reduce-scatter.11.cloned.1.call-update) | async-done | bytes 65552 | tf_op jit(solution)/shard_map/reduce_scatter | solution.py:64
  268.1 5.6 %all_gather.14 = f32[32,1024]{1,0:T(8,128)} all-gather(f32[16,1024]{1,0:T(8,128)} %reduce-scatter.11.cloned.1.call-done), channel_id=1, replica_groups=mesh['blk'=2,'z'=4,'y'=4,'xh'=2,'core'=2] {'xh'}, dimensions={0}, use_global_device_ids=true | all-gather | bytes 196608 | tf_op jit(solution)/shard_map/all_gather | solution.py:66
  273.7 0.0 all-gather.6.cloned.1.call-update
  273.7 0.0 all-gather.8.cloned.1.call-start
  273.7 44.7 %all-gather.6.cloned.1.call-done = f32[512,1024]{1,0:T(8,128)} async-done(((f32[32,1024]{1,0:T(8,128)}), f32[512,1024]{1,0:T(8,128)}) %all-gather.6.cloned.1.call-update) | async-done | bytes 2097168 | tf_op jit(solution)/shard_map/all_gather | solution.py:66
  318.4 0.0 all-gather.8.cloned.1.call-update
  318.5 0.2 reduce-scatter.13.cloned.1.call-start
  318.7 0.0 copy-done
  318.7 0.1 dynamic_slice.7
  318.8 0.3 select_multiply_fusion
  319.1 18.5 %all-gather.8.cloned.1.call-done = f32[1024,1024]{1,0:T(8,128)} async-done(((f32[512,1024]{1,0:T(8,128)}), f32[1024,1024]{1,0:T(8,128)}) %all-gather.8.cloned.1.call-update) | async-done | bytes 4194320 | tf_op jit(solution)/shard_map/all_gather | solution.py:66
  337.6 2.9 broadcast_multiply_fusion
  340.4 0.2 fusion.8
  340.6 1.7 slice_bitcast_fusion.4
  342.3 3.5 maximum_bitcast_fusion
  345.7 4.1 pad_maximum_fusion
  349.8 13.3 %copy.10 = f32[1024,1024,2]{0,2,1:T(2,128)} copy(f32[1024,1024,2]{1,0,2:T(8,128)} %pad_maximum_fusion) | data formatting | bytes 16777216 | tf_op jit(solution)/shard_map/stack | solution.py:36
  363.2 10.9 %reshape.83 = f32[1024,2048]{0,1:T(8,128)} reshape(f32[1024,1024,2]{0,2,1:T(2,128)} %copy.10) | data formatting | bytes 16777216 | tf_op jit(solution)/shard_map/reshape | solution.py:42
  374.1 10.5 %dot_general.12 = f32[1024,2,1024]{2,1,0:T(2,128)} reshape(f32[2048,1024]{1,0:T(8,128)} %bitcast.55) | data formatting | bytes 16777216 | tf_op jit(solution)/shard_map/dot_general | solution.py:43
  384.6 33.2 %fusion = f32[1024,2,1024]{2,0,1:T(8,128)S(1)} fusion(f32[1024,1024,1]{1,0,2:T(8,128)} %bitcast.61, f32[1024,2,1024]{2,1,0:T(2,128)} %dot_general.12), kind=kOutput, calls=%fused_computation.1 | convolution fusion | flops 25769803776 | bytes 20971520 | tf_op jit(solution)/shard_map/dot_general | solution.py:43
  417.9 4.7 %fusion.4 = f32[1024]{0:T(1024)S(1)} fusion(f32[1024,2,1024]{2,0,1:T(8,128)S(1)} %fusion, f32[2,1024,1024]{2,1,0:T(8,128)} %all-gather.4.cloned.1.call-done), kind=kLoop, calls=%fused_computation.6 | loop fusion | flops 4193280 | bytes 16781312 | tf_op jit(solution)/shard_map/reduce_sum | solution.py:100
  422.5 1.0 copy.13
  423.6 0.0 reduce-scatter.13.cloned.1.call-update
  423.6 1.2 dynamic-slice_multiply_fusion
  424.9 0.8 copy.12
  425.7 16.0 %reduce-scatter.13.cloned.1.call-done = f32[512,1]{1,0:T(8,128)} async-done(((f32[1024,1]{1,0:T(8,128)}), f32[512,1]{1,0:T(8,128)}) %reduce-scatter.13.cloned.1.call-update) | async-done | bytes 2064
  441.7 1.1 copy.14
  442.7 0.6 broadcast_multiply_fusion.2
  (1 shorter events, 0.0 us)
Async XLA Ops:
  7.2 115.7 %all-gather.4.cloned.1.call-start = ((), (), s32[]{:S(2)}) async-start(), calls=%async_computation.4 | async-start | bytes 12582912 | tf_op jit(solution)/shard_map/all_gather | solution.py:90
  13.1 0.7 copy-start.1
  13.2 159.5 %reduce-scatter.7.cloned.1.call-start = ((), (), s32[]{:S(2)}) async-start(), calls=%async_computation.5 | async-start | bytes 6291456 | tf_op jit(solution)/shard_map/reduce_scatter | solution.py:64
  156.2 162.5 %copy-start = (s32[1024]{0:T(1024)S(1)}, s32[1024]{0:T(1024)}, u32[]{:S(2)}) copy-start(s32[1024]{0:T(1024)} %param.9) | copy-start | bytes 12292
  156.3 94.6 %reduce-scatter.9.cloned.1.call-start = ((), (), s32[]{:S(2)}) async-start(), calls=%async_computation.6 | async-start | bytes 2228224 | tf_op jit(solution)/shard_map/reduce_scatter | solution.py:64
  172.7 95.4 %reduce-scatter.11.cloned.1.call-start = ((), (), s32[]{:S(2)}) async-start(), calls=%async_computation.7 | async-start | bytes 196608 | tf_op jit(solution)/shard_map/reduce_scatter | solution.py:64
  250.9 67.6 %all-gather.6.cloned.1.call-start = ((), (), s32[]{:S(2)}) async-start(), calls=%async_computation.8 | async-start | bytes 2228224 | tf_op jit(solution)/shard_map/all_gather | solution.py:66
  273.7 63.9 %all-gather.8.cloned.1.call-start = ((), (), s32[]{:S(2)}) async-start(), calls=%async_computation.9 | async-start | bytes 6291456 | tf_op jit(solution)/shard_map/all_gather | solution.py:66
  318.5 123.2 %reduce-scatter.13.cloned.1.call-start = ((), (), s32[]{:S(2)}) async-start(), calls=%async_computation.10 | async-start | bytes 786432
Sparse Core Ops, SparseCore 0:
  13.3 109.5 all-gather.3
  156.4 16.2 reduce-scatter.6
  176.0 74.8 reduce-scatter.8
  253.0 14.9 reduce-scatter.10
  273.8 44.5 all-gather.5
  320.0 17.5 all-gather.7
  423.7 17.8 reduce-scatter.12
